TPU v7x, 512 devices: a whole 4x8x8 slice. The times are simulated.
512 devices in a mesh: dp: 32 (over y, x), tensor: 16 (over z, core).
Axes of the slice: x: 4, y: 8, z: 8, core: 2. Of those that a mesh axis runs over, the one named last changes fastest.
Arguments:
- patch_rows: bfloat16 [32, 3072, 1792], P('dp', 'tensor'), may hold values from -6 to 6
- send_rows: int32 [32, 16, 32, 6], P('dp', 'tensor'), may hold values from 0 to 192, as said below
- take_rows: int32 [32, 2048], P('dp', 'tensor'), may hold values from 0 to 191, as said below
- segments: int32 [32, 2048], P('dp', 'tensor'), may hold values from 0 to 41, never falling along the last dimension, each value on 1 to 96 neighbouring positions
- norm_gain: float32 [1792], replicated, may hold values from 0.5 to 5
- qkv_weight: bfloat16 [1792, 2688], P('tensor'), may hold values from -0.125 to 0.125
- out_weight: bfloat16 [896, 1792], P('tensor'), may hold values from -0.1875 to 0.1875
- grad_out: bfloat16 [32, 2048, 1792], P('dp', 'tensor'), may hold values from -6 to 6
Outputs:
- layer_out: bfloat16 [32, 2048, 1792], P('dp', 'tensor')
- patch_grad: bfloat16 [32, 3072, 1792], P('dp', 'tensor')
Inputs may be any that keep to these rules, and one draw needn't show every extreme that they name: `send_rows`: for each source device (s, t) the entries below 192 are distinct, 128 in all; for each group they fill slots from 0 on, the rest being 192; some device sends 6 rows to some group. `take_rows`: for each g and t the 128 entries are distinct and name exactly the slots s * 6 + c that hold a row (c below the number of rows that device (s, t) sends to group g). `segments`: along each row the ids never fall and each id covers 1 to 96 positions.
All inputs are finite; a program needn't handle non-finite values.
Results may differ from a plain program's by a relative error of at most 0.009.
The roundings to bfloat16 on the way count: a program that leaves them out, or rounds other values in their place, can miss the bound.
Values may be sent and summed in bfloat16 or wider, within the bound.
No kernel may reach another device: no remote copies, remote signals or barrier semaphores. Data moves between devices by JAX's collectives and lax.ppermute only.
A program may use at most 128 MiB of HBM per device.

v0:
```python
import jax
import jax.numpy as jnp
from jax import lax
from jax.sharding import PartitionSpec as P

HD = 112
HEADS = 8
MOST = 96


def extended(block, sides, width):
    for axis, dim in sides:
        count = lax.axis_size(axis)
        forward = [(i, i + 1) for i in range(count - 1)]
        backward = [(target, source) for source, target in forward]
        low = lax.ppermute(
            lax.slice_in_dim(block, block.shape[dim] - width, None, axis=dim), axis, forward
        )
        high = lax.ppermute(lax.slice_in_dim(block, 0, width, axis=dim), axis, backward)
        block = jnp.concatenate([low, block, high], axis=dim)
    return block


def gather_weights(qkv_weight, out_weight):
    qkv_rows, qkv_cols = qkv_weight.shape
    out_rows, out_cols = out_weight.shape
    out_wide = out_weight.reshape(qkv_rows, out_rows * out_cols // qkv_rows)
    both = lax.all_gather(
        jnp.concatenate([qkv_weight, out_wide], axis=1), "tensor", axis=0, tiled=True
    )
    full_qkv = both[:, :qkv_cols]
    out_pairs = both[:, qkv_cols:]
    return (full_qkv, out_pairs)


def spread(cols, side):
    rows = cols.shape[0]
    none = jnp.zeros_like(cols)
    pair = (cols, none) if side == 0 else (none, cols)
    return jnp.stack(pair, axis=-1).reshape(rows, 2 * cols.shape[1])


def times_out(attended, out_pairs):
    halves = [
        jnp.dot(spread(attended, side), out_pairs, preferred_element_type=jnp.float32)
        for side in range(2)
    ]
    return jnp.concatenate(halves, axis=1)


def times_out_t(grad_rows, out_pairs):
    half = out_pairs.shape[1]
    rows = grad_rows.shape[0]
    parts = [
        lax.dot_general(
            grad_rows[:, side * half : (side + 1) * half],
            out_pairs,
            (((1,), (1,)), ((), ())),
            preferred_element_type=jnp.float32,
        )
        for side in range(2)
    ]
    even = lax.broadcasted_iota(jnp.int32, parts[0].shape, 1) % 2 == 0
    return jnp.where(even, parts[0], parts[1]).reshape(rows, -1, 2).sum(axis=2)


def normalize(rows_in, norm_gain):
    values = rows_in.astype(jnp.float32)
    center = values - jnp.mean(values, axis=-1, keepdims=True)
    inv_dev = lax.rsqrt(jnp.mean(center * center, axis=-1, keepdims=True) + 1e-06)
    unit_rows = center * inv_dev
    return (values, unit_rows, inv_dev, (unit_rows * norm_gain).astype(jnp.bfloat16))


def head_blocks(rows_in, count):
    tiled = jnp.tile(rows_in, (HEADS, 1))
    row_head = lax.broadcasted_iota(jnp.int32, tiled.shape, 0) // count
    col_head = lax.broadcasted_iota(jnp.int32, tiled.shape, 1) // HD
    return jnp.where(row_head == col_head, tiled, jnp.zeros_like(tiled))


def own_heads(stacked, count):
    row_head = lax.broadcasted_iota(jnp.int32, stacked.shape, 0) // count
    col_head = lax.broadcasted_iota(jnp.int32, stacked.shape, 1) // HD
    kept = jnp.where(row_head == col_head, stacked, jnp.zeros_like(stacked))
    return kept.reshape(HEADS, count, stacked.shape[1]).sum(axis=0)


def rows_dot(a, b):
    return lax.dot_general(a, b, (((1,), (1,)), ((), ())), preferred_element_type=jnp.float32)


def cols_dot(a, b):
    return lax.dot_general(a, b, (((0,), (0,)), ((), ())), preferred_element_type=jnp.float32)


def attend(queries, keyval, seg_query, seg_key):
    all_heads = HEADS * HD
    score_scale = HD ** (-0.5)
    count = queries.shape[0]
    query_blocks = head_blocks(queries, count)
    scores = rows_dot(query_blocks, keyval[:, :all_heads]) * score_scale
    same_chart = jnp.tile(seg_query[:, None] == seg_key[None, :], (HEADS, 1))
    scores = jnp.where(same_chart, scores, -jnp.inf)
    row_max = jnp.max(scores, axis=1, keepdims=True)
    exp_scores = jnp.exp(scores - row_max)
    row_sum = jnp.sum(exp_scores, axis=1, keepdims=True)
    attn_probs = exp_scores / row_sum
    prob_low = attn_probs.astype(jnp.bfloat16)
    mixed = jnp.dot(prob_low, keyval[:, all_heads:], preferred_element_type=jnp.float32)
    attended = own_heads(mixed, count)
    return (attn_probs, prob_low, attended.astype(jnp.bfloat16), query_blocks)


def local(patch_rows, send_rows, take_rows, segments, norm_gain, qkv_weight, out_weight, grad_out):
    groups = lax.axis_size("dp")
    src_count = patch_rows.shape[1]
    features = patch_rows.shape[2]
    slot_count = send_rows.shape[3]
    own_rows = take_rows.shape[1]
    all_heads = HEADS * HD
    score_scale = HD ** (-0.5)
    patches = patch_rows[0]
    send_flat = send_rows.reshape(groups * slot_count)
    outgoing = jnp.take(patches, send_flat, axis=0, mode="fill", fill_value=0).reshape(
        groups, slot_count, features
    )
    incoming = lax.all_to_all(outgoing, "dp", split_axis=0, concat_axis=0, tiled=True).reshape(
        groups * slot_count, features
    )
    pick_rows = take_rows[0]
    slot_total = groups * slot_count
    row_slot = (
        jnp.full((src_count + 1,), slot_total, jnp.int32)
        .at[send_flat]
        .set(jnp.arange(slot_total, dtype=jnp.int32))[:src_count]
    )
    packed = jnp.take(incoming, pick_rows, axis=0)
    full_qkv, full_out = gather_weights(qkv_weight, out_weight)
    values, unit_rows, inv_dev, normed = normalize(packed, norm_gain)
    projected = jnp.dot(normed, full_qkv, preferred_element_type=jnp.float32).astype(jnp.bfloat16)
    queries = projected[:, :all_heads]
    keyval = projected[:, all_heads:]
    seg_plus = segments[0] + 1
    wide_kv, wide_seg = (
        extended(keyval, (("tensor", 0),), MOST),
        extended(seg_plus, (("tensor", 0),), MOST),
    )
    attn_probs, prob_low, attended, query_blocks = attend(queries, wide_kv, seg_plus, wide_seg)
    layer_out = (values + times_out(attended, full_out)).astype(jnp.bfloat16)
    grad_rows = grad_out[0]
    grad_att = times_out_t(grad_rows, full_out).astype(jnp.bfloat16)
    grad_blocks = head_blocks(grad_att, own_rows)
    dprobs = rows_dot(grad_blocks, wide_kv[:, all_heads:])
    row_inner = jnp.sum(attn_probs * dprobs, axis=1, keepdims=True)
    dscore = (attn_probs * (dprobs - row_inner) * score_scale).astype(jnp.bfloat16)
    window_rows = wide_kv.shape[0]
    score_rows = dscore.reshape(HEADS, own_rows, window_rows).transpose(1, 0, 2)
    grad_query = jnp.dot(
        score_rows.reshape(own_rows, HEADS * window_rows),
        head_blocks(wide_kv[:, :all_heads], window_rows),
        preferred_element_type=jnp.float32,
    )
    grad_key = cols_dot(dscore, query_blocks)
    grad_value = cols_dot(prob_low, grad_blocks)
    grad_window = jnp.concatenate([grad_key, grad_value], axis=1)
    center = grad_window[MOST : MOST + own_rows]
    blocks = lax.axis_size("tensor")
    ahead = [(i, i + 1) for i in range(blocks - 1)]
    behind = [(target, source) for source, target in ahead]
    high_rim, low_rim = lax.optimization_barrier(
        (grad_window[MOST + own_rows :], grad_window[:MOST])
    )
    from_prev = lax.ppermute(high_rim, "tensor", ahead)
    from_next = lax.ppermute(low_rim, "tensor", behind)
    center = center.at[:MOST].add(from_prev)
    center = center.at[own_rows - MOST :].add(from_next)
    grad_proj = jnp.concatenate([grad_query, center], axis=1).astype(jnp.bfloat16)
    grad_normed = lax.dot_general(
        grad_proj, full_qkv, (((1,), (1,)), ((), ())), preferred_element_type=jnp.float32
    )
    scaled = grad_normed * norm_gain
    grad_unit = (
        scaled
        - jnp.mean(scaled, axis=-1, keepdims=True)
        - unit_rows * jnp.mean(scaled * unit_rows, axis=-1, keepdims=True)
    )
    grad_packed = (grad_rows.astype(jnp.float32) + inv_dev * grad_unit).astype(jnp.bfloat16)
    back_slots = (
        jnp.zeros((groups * slot_count, features), jnp.bfloat16).at[pick_rows].set(grad_packed)
    )
    back_slots = back_slots.reshape(groups, slot_count, features)
    returned = lax.all_to_all(back_slots, "dp", split_axis=0, concat_axis=0, tiled=True).reshape(
        groups * slot_count, features
    )
    patch_grad = jnp.take(returned, row_slot, axis=0, mode="fill", fill_value=0)
    return (layer_out[None], patch_grad[None])


def solution(mesh):
    return jax.shard_map(
        local,
        mesh=mesh,
        in_specs=(
            P("dp", "tensor", None),
            P("dp", "tensor", None, None),
            P("dp", "tensor"),
            P("dp", "tensor"),
            P(),
            P("tensor", None),
            P("tensor", None),
            P("dp", "tensor", None),
        ),
        out_specs=(P("dp", "tensor", None), P("dp", "tensor", None)),
        check_vma=False,
    )
```

profile of v0, /device:TPU:66, one launch (start us, length us, event | category | flops | bytes accessed | tf_op | source)
XLA Modules:
  0.0 185.1 jit_solution(1266978088564810541)
XLA Ops:
  7.2 1.1 reshape.392
  8.3 2.0 %pad_maximum_fusion.1 = bf16[112,3584]{1,0:T(8,128)(2,1)} fusion(bf16[112,896]{1,0:T(8,128)(2,1)S(1)} %reshape.392, bf16[112,2688]{1,0:T(8,128)(2,1)} %param.19), kind=kLoop, calls=%fused_computation.67 | loop fusion | flops 1605632 | bytes 1605632 | tf_op jit(solution)/shard_map/concatenate | solution.py:29
  10.6 1.1 gather_fusion.1
  11.9 1.2 reshape.390
  13.1 10.2 %all-to-all-start = ((bf16[32,6,1792]{2,1,0:T(8,128)(2,1)}), bf16[32,6,1792]{2,1,0:T(8,128)(2,1)S(1)}, u32[]{:S(2)}, u32[]{:S(2)}) async-start(bf16[32,6,1792]{2,1,0:T(8,128)(2,1)} %reshape.390), calls=%async_computation | async-start | bytes 1835008 | tf_op jit(solution)/shard_map/all_to_all | solution.py:128
  23.4 1.9 %collective-permute-start = (s32[96]{0:T(128)S(1)}, s32[96]{0:T(128)S(1)}, u32[]{:S(2)}, u32[]{:S(2)}) collective-permute-start(s32[96]{0:T(128)S(1)} %get-tuple-element.41), channel_id=1, source_target_pairs={{0,1},{1,2},{2,3},{3,4},{4,5},{5,6},{6,7},{7,8},{8,9},{9,10},{10,1... | collective-permute-start | bytes 1160 | tf_op jit(solution)/shard_map/ppermute | solution.py:16
  25.3 3.6 %collective-permute-start.1 = (s32[96]{0:T(128)S(1)}, s32[96]{0:T(128)S(1)}, u32[]{:S(2)}, u32[]{:S(2)}) collective-permute-start(s32[96]{0:T(128)S(1)} %get-tuple-element.42), channel_id=1, source_target_pairs={{1,0},{2,1},{3,2},{4,3},{5,4},{6,5},{7,6},{8,7},{9,8},{10,9},{11,1... | collective-permute-start | bytes 1160 | tf_op jit(solution)/shard_map/ppermute | solution.py:19
  29.1 1.2 scatter_custom_fusion.1
  38.8 9.7 %all-to-all-done = bf16[32,6,1792]{2,1,0:T(8,128)(2,1)S(1)} async-done(((bf16[32,6,1792]{2,1,0:T(8,128)(2,1)}), bf16[32,6,1792]{2,1,0:T(8,128)(2,1)S(1)}, u32[]{:S(2)}, u32[]{:S(2)}) %all-to-all-start) | async-done | bytes 688160 | tf_op jit(solution)/shard_map/all_to_all | solution.py:128
  50.3 42.0 %all-gather.2.cloned.1.call-done = bf16[1792,3584]{1,0:T(8,128)(2,1)} async-done(((bf16[112,3584]{1,0:T(8,128)(2,1)}), bf16[1792,3584]{1,0:T(8,128)(2,1)}) %all-gather.2.cloned.1.call-update) | async-done | bytes 12845072 | tf_op jit(solution)/shard_map/all_gather | solution.py:28
  92.3 5.5 %fusion.9 = bf16[128,2688]{1,0:T(8,128)(2,1)S(1)} fusion(bf16[1792,3584]{1,0:T(8,128)(2,1)} %all-gather.2.cloned.1.call-done, f32[1792]{0:T(1024)S(1)} %copy-done.27, f32[128]{0:T(128)S(1)} %add_rsqrt_fusion, f32[128]{0:T(128)S(1)} %broadcast_multiply_fusion.2, bf16[128,1792]{1,0:T(8,128)(2,1)S(1)} %gather_fusion, pred[128]{0:T(512)(128)(4,1)S(1)} %compare_and_fusion.2), kind=kOutput, calls=%fused_computation.15 | convolution fusion | flops 1234845696 | bytes 10788992 | tf_op jit(solution)/shard_map/dot_general | solution.py:141
  98.7 2.3 %collective-permute-start.2 = (bf16[96,1792]{1,0:T(8,128)(2,1)}, bf16[96,1792]{1,0:T(8,128)(2,1)S(1)}, u32[]{:S(2)}, u32[]{:S(2)}) collective-permute-start(bf16[96,1792]{1,0:T(8,128)(2,1)} %get-tuple-element.35), channel_id=1, source_target_pairs={{0,1},{1,2},{2,3},{3,4},{4,5},{5,6},{6,7},{7,8},{8,9},{9,10},{10,1... | collective-permute-start | bytes 1032200 | tf_op jit(solution)/shard_map/ppermute | solution.py:16
  101.0 4.5 %collective-permute-start.3 = (bf16[96,1792]{1,0:T(8,128)(2,1)S(1)}, bf16[96,1792]{1,0:T(8,128)(2,1)S(1)}, u32[]{:S(2)}, u32[]{:S(2)}) collective-permute-start(bf16[96,1792]{1,0:T(8,128)(2,1)S(1)} %get-tuple-element.36), channel_id=1, source_target_pairs={{1,0},{2,1},{3,2},{4,3},{5,4},{6,5},{7,6},{8,7},{9,8},{10,9},{11,1... | collective-permute-start | bytes 1032200 | tf_op jit(solution)/shard_map/ppermute | solution.py:19
  107.7 1.2 reduce_sum.76
  109.1 1.8 fusion.18
  116.3 2.1 %collective-permute-start.4 = (f32[96,1792]{1,0:T(8,128)S(1)}, f32[96,1792]{1,0:T(8,128)S(1)}, u32[]{:S(2)}, u32[]{:S(2)}) collective-permute-start(f32[96,1792]{1,0:T(8,128)S(1)} %get-tuple-element.29), channel_id=1, source_target_pairs={{0,1},{1,2},{2,3},{3,4},{4,5},{5,6},{6,7},{7,8},{8,9},{9,10},{10,1... | collective-permute-start | bytes 2064392 | tf_op jit(solution)/shard_map/ppermute | solution.py:174
  118.3 3.9 %collective-permute-start.5 = (f32[96,1792]{1,0:T(8,128)S(1)}, f32[96,1792]{1,0:T(8,128)S(1)}, u32[]{:S(2)}, u32[]{:S(2)}) collective-permute-start(f32[96,1792]{1,0:T(8,128)S(1)} %get-tuple-element.30), channel_id=1, source_target_pairs={{1,0},{2,1},{3,2},{4,3},{5,4},{6,5},{7,6},{8,7},{9,8},{10,9},{11,1... | collective-permute-start | bytes 2064392 | tf_op jit(solution)/shard_map/ppermute | solution.py:175
  122.3 1.8 fusion.37
  124.2 4.5 %collective-permute-done.4 = f32[96,1792]{1,0:T(8,128)S(1)} collective-permute-done((f32[96,1792]{1,0:T(8,128)S(1)}, f32[96,1792]{1,0:T(8,128)S(1)}, u32[]{:S(2)}, u32[]{:S(2)}) %collective-permute-start.4) | collective-permute-done | bytes 688160 | tf_op jit(solution)/shard_map/ppermute | solution.py:174
  128.8 1.6 collective-permute-done.5
  130.7 3.7 %fusion.106 = (f32[128]{0:T(128)S(1)}, f32[128]{0:T(128)S(1)}, f32[128,1792]{1,0:T(8,128)}) fusion(f32[128]{0:T(128)S(1)} %copy-done.26, f32[128]{0:T(128)S(1)} %copy-done.20, bf16[128,1792]{1,0:T(8,128)(2,1)S(1)} %gather_fusion, pred[128]{0:T(512)(128)(4,1)S(1)} %copy-done.16, f32[1792]{0:T(1024)S(1)} %copy-done.28, bf16[1792,3584]{1,0:T(8,128)(2,1)S(1)} %bitcast.76, ...), kind=kOutput, calls=%fused_computation.154 | convolution fusion | flops 1236336384 | bytes 11708928 | tf_op jit(solution)/shard_map/dot_general | solution.py:179
  134.4 2.6 %scatter_custom_fusion = bf16[192,1792]{1,0:T(8,128)(2,1)S(1)} fusion(s32[128]{0:T(128)} %copy-done.24, f32[128,1792]{1,0:T(8,128)} %get-tuple-element.49, f32[128]{0:T(128)S(1)} %broadcast_multiply_fusion, f32[128]{0:T(128)S(1)} %broadcast_multiply_fusion.1, f32[128]{0:T(128)S(1)} %copy-done.26, f32[128]{0:T(128)S(1)} %copy-done.20, ...), kind=kCustom, calls=%fused_computation.84 | custom fusion | flops 2523136 | bytes 2525824 | tf_op jit(solution)/shard_map/scatter | solution.py:190
  137.1 1.2 reshape.398
  138.2 9.9 %all-to-all-start.1 = ((bf16[32,6,1792]{2,1,0:T(8,128)(2,1)}), bf16[32,6,1792]{2,1,0:T(8,128)(2,1)}, u32[]{:S(2)}, u32[]{:S(2)}) async-start(bf16[32,6,1792]{2,1,0:T(8,128)(2,1)} %reshape.398), calls=%async_computation.1 | async-start | bytes 1835008 | tf_op jit(solution)/shard_map/all_to_all | solution.py:193
  148.2 3.8 %fusion.19 = f32[1024,896]{1,0:T(8,128)} fusion(s32[896]{0:T(1024)S(1)} %copy-done.9, s32[896]{0:T(1024)S(1)} %copy-done.10, s32[1024]{0:T(1024)S(1)} %copy-done.11, s32[1024]{0:T(1024)S(1)} %copy-done.12, pred[1024]{0:T(1024)(128)(4,1)S(1)} %copy-done.22, pred[896]{0:T(1024)(128)(4,1)S(1)} %copy-done.21, bf16[320,1792]{1,0:T(8,128)(2,1)} %copy-done.3, ...), kind=kOutput, calls=%fused_computation.29 | convolution fusion | flops 591855616 | bytes 5579648 | tf_op jit(solution)/shard_map/dot_general | solution.py:110
  152.0 2.2 %reduce_sum.75 = bf16[128,896]{1,0:T(8,128)(2,1)S(1)} reduce(f32[8,128,896]{2,1,0:T(8,128)} %bitcast.74, f32[]{:T(128)} %constant.161.clone.1), dimensions={0}, to_apply=%region_4.6 | reduce | flops 802816 | bytes 3899396 | tf_op jit(solution)/shard_map/reduce_sum | solution.py:86
  155.0 1.1 fusion.108
  156.2 2.6 %fusion.28 = f32[1,128,896]{2,1,0:T(8,128)S(1)} fusion(bf16[128,1792]{0,1:T(8,128)(2,1)S(1)} %bitcast.79, bf16[1792,3584]{1,0:T(8,128)(2,1)} %all-gather.2.cloned.1.call-done), kind=kOutput, calls=%fused_computation.42 | convolution fusion | flops 411041792 | bytes 4128768 | tf_op jit(solution)/shard_map/dot_general | solution.py:45
  158.8 2.6 %fusion.31 = f32[1,128,896]{2,1,0:T(8,128)S(1)} fusion(bf16[128,1792]{0,1:T(8,128)(2,1)S(1)} %bitcast.78, bf16[1792,3584]{1,0:T(8,128)(2,1)} %all-gather.2.cloned.1.call-done), kind=kOutput, calls=%fused_computation.43 | convolution fusion | flops 411041792 | bytes 4128768 | tf_op jit(solution)/shard_map/dot_general | solution.py:45
  162.3 12.3 %all-to-all-done.1 = bf16[32,6,1792]{2,1,0:T(8,128)(2,1)} async-done(((bf16[32,6,1792]{2,1,0:T(8,128)(2,1)}), bf16[32,6,1792]{2,1,0:T(8,128)(2,1)}, u32[]{:S(2)}, u32[]{:S(2)}) %all-to-all-start.1) | async-done | bytes 688160 | tf_op jit(solution)/shard_map/all_to_all | solution.py:193
  174.6 1.4 reshape.399
  176.0 1.3 gather_fusion.2
  (143 shorter events, 22.2 us)
Async XLA Ops:
  7.2 85.1 %all-gather.2.cloned.1.call-start = ((), (), s32[]{:S(2)}) async-start(), calls=%async_computation.2 | async-start | bytes 13647872 | tf_op jit(solution)/shard_map/all_gather | solution.py:28
  11.9 11.4 %copy-start.29 = (s32[1,128]{1,0:T(1,128)S(1)}, s32[1,128]{1,0:T(1,128)}, u32[]{:S(2)}) copy-start(s32[1,128]{1,0:T(1,128)} %param.17) | copy-start | bytes 1540
  11.9 19.0 %copy-start.30 = (s32[1,128]{1,0:T(1,128)S(1)}, s32[1,128]{1,0:T(1,128)}, u32[]{:S(2)}) copy-start(s32[1,128]{1,0:T(1,128)} %param.16) | copy-start | bytes 1540
  13.1 35.5 %all-to-all-start = ((bf16[32,6,1792]{2,1,0:T(8,128)(2,1)}), bf16[32,6,1792]{2,1,0:T(8,128)(2,1)S(1)}, u32[]{:S(2)}, u32[]{:S(2)}) async-start(bf16[32,6,1792]{2,1,0:T(8,128)(2,1)} %reshape.390), calls=%async_computation | async-start | bytes 1835008 | tf_op jit(solution)/shard_map/all_to_all | solution.py:128
  23.4 14.6 %collective-permute-start = (s32[96]{0:T(128)S(1)}, s32[96]{0:T(128)S(1)}, u32[]{:S(2)}, u32[]{:S(2)}) collective-permute-start(s32[96]{0:T(128)S(1)} %get-tuple-element.41), channel_id=1, source_target_pairs={{0,1},{1,2},{2,3},{3,4},{4,5},{5,6},{6,7},{7,8},{8,9},{9,10},{10,1... | collective-permute-start | bytes 1160 | tf_op jit(solution)/shard_map/ppermute | solution.py:16
  25.3 12.7 %collective-permute-start.1 = (s32[96]{0:T(128)S(1)}, s32[96]{0:T(128)S(1)}, u32[]{:S(2)}, u32[]{:S(2)}) collective-permute-start(s32[96]{0:T(128)S(1)} %get-tuple-element.42), channel_id=1, source_target_pairs={{1,0},{2,1},{3,2},{4,3},{5,4},{6,5},{7,6},{8,7},{9,8},{10,9},{11,1... | collective-permute-start | bytes 1160 | tf_op jit(solution)/shard_map/ppermute | solution.py:19
  34.6 57.7 %copy-start.15 = (pred[128]{0:T(512)(128)(4,1)}, pred[128]{0:T(512)(128)(4,1)S(1)}, u32[]{:S(2)}) copy-start(pred[128]{0:T(512)(128)(4,1)S(1)} %compare_and_fusion.2) | copy-start | bytes 388
  48.8 43.5 %copy-start.27 = (f32[1792]{0:T(1024)S(1)}, f32[1792]{0:T(1024)}, u32[]{:S(2)}) copy-start(f32[1792]{0:T(1024)} %param.18) | copy-start | bytes 21508
  50.0 47.9 %copy-start.19 = (f32[128]{0:T(128)}, f32[128]{0:T(128)S(1)}, u32[]{:S(2)}) copy-start(f32[128]{0:T(128)S(1)} %broadcast_multiply_fusion.2) | copy-start | bytes 1540
  50.3 47.6 %copy-start.25 = (f32[128]{0:T(128)}, f32[128]{0:T(128)S(1)}, u32[]{:S(2)}) copy-start(f32[128]{0:T(128)S(1)} %add_rsqrt_fusion) | copy-start | bytes 1540
  92.3 13.2 %copy-start.1 = (bf16[1792,3584]{1,0:T(8,128)(2,1)S(1)}, bf16[1792,3584]{1,0:T(8,128)(2,1)}, u32[]{:S(2)}) copy-start(bf16[1792,3584]{1,0:T(8,128)(2,1)} %all-gather.2.cloned.1.call-done) | copy-start | bytes 38535172
  97.9 8.7 %copy-start.2 = (bf16[128,2688]{1,0:T(8,128)(2,1)}, bf16[128,2688]{1,0:T(8,128)(2,1)S(1)}, u32[]{:S(2)}) copy-start(bf16[128,2688]{1,0:T(8,128)(2,1)S(1)} %fusion.9) | copy-start | bytes 2064388
  97.9 7.6 %copy-start.4 = (bf16[1,128,1792]{2,1,0:T(8,128)(2,1)S(1)}, bf16[1,128,1792]{2,1,0:T(8,128)(2,1)}, u32[]{:S(2)}) copy-start(bf16[1,128,1792]{2,1,0:T(8,128)(2,1)} %param.21) | copy-start | bytes 1376260
  98.7 12.2 %collective-permute-start.2 = (bf16[96,1792]{1,0:T(8,128)(2,1)}, bf16[96,1792]{1,0:T(8,128)(2,1)S(1)}, u32[]{:S(2)}, u32[]{:S(2)}) collective-permute-start(bf16[96,1792]{1,0:T(8,128)(2,1)} %get-tuple-element.35), channel_id=1, source_target_pairs={{0,1},{1,2},{2,3},{3,4},{4,5},{5,6},{6,7},{7,8},{8,9},{9,10},{10,1... | collective-permute-start | bytes 1032200 | tf_op jit(solution)/shard_map/ppermute | solution.py:16
  101.0 9.9 %collective-permute-start.3 = (bf16[96,1792]{1,0:T(8,128)(2,1)S(1)}, bf16[96,1792]{1,0:T(8,128)(2,1)S(1)}, u32[]{:S(2)}, u32[]{:S(2)}) collective-permute-start(bf16[96,1792]{1,0:T(8,128)(2,1)S(1)} %get-tuple-element.36), channel_id=1, source_target_pairs={{1,0},{2,1},{3,2},{4,3},{5,4},{6,5},{7,6},{8,7},{9,8},{10,9},{11,1... | collective-permute-start | bytes 1032200 | tf_op jit(solution)/shard_map/ppermute | solution.py:19
  116.1 6.1 %slice-start.6 = ((bf16[320,1792]{1,0:T(8,128)(2,1)}), bf16[320,896]{1,0:T(8,128)(2,1)S(1)}, s32[]{:S(2)}) async-start(bf16[320,1792]{1,0:T(8,128)(2,1)} %copy-done.3), calls=%async_computation.9 | async-start | bytes 1146880 | tf_op jit(solution)/shard_map/slice | solution.py:102
  116.1 6.1 %copy-start.5 = (s32[8,320]{0,1:T(8,128)S(1)}, s32[8,320]{0,1:T(8,128)}, u32[]{:S(2)}) copy-start(s32[8,320]{0,1:T(8,128)} %copy.27) | copy-start | bytes 30724
  116.1 6.1 %copy-start.6 = (s32[8,320]{0,1:T(8,128)S(1)}, s32[8,320]{0,1:T(8,128)}, u32[]{:S(2)}) copy-start(s32[8,320]{0,1:T(8,128)} %copy.28) | copy-start | bytes 30724
  116.1 6.1 %copy-start.8 = (pred[8,320]{0,1:T(8,128)(4,1)S(1)}, pred[8,320]{0,1:T(8,128)(4,1)}, u32[]{:S(2)}) copy-start(pred[8,320]{0,1:T(8,128)(4,1)} %copy.26) | copy-start | bytes 7684
  116.2 6.1 %copy-start.9 = (s32[896]{0:T(1024)S(1)}, s32[896]{0:T(1024)}, u32[]{:S(2)}) copy-start(s32[896]{0:T(1024)} %get-tuple-element.52) | copy-start | bytes 10756
  116.2 6.1 %copy-start.10 = (s32[896]{0:T(1024)S(1)}, s32[896]{0:T(1024)}, u32[]{:S(2)}) copy-start(s32[896]{0:T(1024)} %get-tuple-element.53) | copy-start | bytes 10756
  116.2 6.1 %copy-start.21 = (pred[896]{0:T(1024)(128)(4,1)S(1)}, pred[896]{0:T(1024)(128)(4,1)}, u32[]{:S(2)}) copy-start(pred[896]{0:T(1024)(128)(4,1)} %fusion.94) | copy-start | bytes 2692
  116.3 12.4 %collective-permute-start.4 = (f32[96,1792]{1,0:T(8,128)S(1)}, f32[96,1792]{1,0:T(8,128)S(1)}, u32[]{:S(2)}, u32[]{:S(2)}) collective-permute-start(f32[96,1792]{1,0:T(8,128)S(1)} %get-tuple-element.29), channel_id=1, source_target_pairs={{0,1},{1,2},{2,3},{3,4},{4,5},{5,6},{6,7},{7,8},{8,9},{9,10},{10,1... | collective-permute-start | bytes 2064392 | tf_op jit(solution)/shard_map/ppermute | solution.py:174
  118.3 12.1 %collective-permute-start.5 = (f32[96,1792]{1,0:T(8,128)S(1)}, f32[96,1792]{1,0:T(8,128)S(1)}, u32[]{:S(2)}, u32[]{:S(2)}) collective-permute-start(f32[96,1792]{1,0:T(8,128)S(1)} %get-tuple-element.30), channel_id=1, source_target_pairs={{1,0},{2,1},{3,2},{4,3},{5,4},{6,5},{7,6},{8,7},{9,8},{10,9},{11,1... | collective-permute-start | bytes 2064392 | tf_op jit(solution)/shard_map/ppermute | solution.py:175
  122.3 8.3 %slice-start = ((s8[12845056]{0:T(1024)(128)(4,1)}), s8[4194304]{0:T(1024)(128)(4,1)S(1)}, s32[]{:S(2)}) async-start(s8[12845056]{0:T(1024)(128)(4,1)} %bitcast.75), calls=%async_computation.3 | async-start | bytes 8388608
  122.3 8.3 %slice-start.1 = ((s8[12845056]{0:T(1024)(128)(4,1)}), s8[4194304]{0:T(1024)(128)(4,1)S(1)}, s32[]{:S(2)}) async-start(s8[12845056]{0:T(1024)(128)(4,1)} %bitcast.75), calls=%async_computation.4 | async-start | bytes 8388608
  122.3 8.3 %slice-start.2 = ((s8[12845056]{0:T(1024)(128)(4,1)}), s8[4194304]{0:T(1024)(128)(4,1)S(1)}, s32[]{:S(2)}) async-start(s8[12845056]{0:T(1024)(128)(4,1)} %bitcast.75), calls=%async_computation.5 | async-start | bytes 8388608
  124.1 6.5 %slice-start.3 = ((s8[12845056]{0:T(1024)(128)(4,1)}), s8[262144]{0:T(1024)(128)(4,1)S(1)}, s32[]{:S(2)}) async-start(s8[12845056]{0:T(1024)(128)(4,1)} %bitcast.75), calls=%async_computation.6 | async-start | bytes 524288
  137.1 11.1 %copy-start.11 = (s32[1024]{0:T(1024)S(1)}, s32[1024]{0:T(1024)}, u32[]{:S(2)}) copy-start(s32[1024]{0:T(1024)} %get-tuple-element.54) | copy-start | bytes 12292
  137.1 11.1 %copy-start.12 = (s32[1024]{0:T(1024)S(1)}, s32[1024]{0:T(1024)}, u32[]{:S(2)}) copy-start(s32[1024]{0:T(1024)} %get-tuple-element.55) | copy-start | bytes 12292
  137.1 11.1 %copy-start.22 = (pred[1024]{0:T(1024)(128)(4,1)S(1)}, pred[1024]{0:T(1024)(128)(4,1)}, u32[]{:S(2)}) copy-start(pred[1024]{0:T(1024)(128)(4,1)} %fusion.95) | copy-start | bytes 3076
  138.2 36.4 %all-to-all-start.1 = ((bf16[32,6,1792]{2,1,0:T(8,128)(2,1)}), bf16[32,6,1792]{2,1,0:T(8,128)(2,1)}, u32[]{:S(2)}, u32[]{:S(2)}) async-start(bf16[32,6,1792]{2,1,0:T(8,128)(2,1)} %reshape.398), calls=%async_computation.1 | async-start | bytes 1835008 | tf_op jit(solution)/shard_map/all_to_all | solution.py:193
  (15 other events, 26.5 us)
Sparse Core Ops, SparseCore 0:
  10.5 81.8 all-gather.1
where the time goes:
time: 186 us; the launch traced here: 185 us
  waiting for transfers between devices  70.2 us (38%)
  starting transfers between devices  38.5 us (21%)
  matrix products  25.7 us (14%)
  other arithmetic  19.1 us (10%)
  local copies, waits for them, and re-layouts  16.7 us (9%)
  between operations  15 us (8%)
    all_gather x1, waiting for transfers between devices, gather_weights(): lax.all_gather(jnp.concatenate([qkv_weight, out_wide], axis=1), 'tensor',...  42 us
    all_to_all x1, waiting for transfers between devices, local(): lax.all_to_all(back_slots, 'dp', split_axis=0, concat_axis=0, tiled=True)  12.3 us
    all_to_all x1, starting transfers between devices, local(): lax.all_to_all(outgoing, 'dp', split_axis=0, concat_axis=0, tiled=True)  10.2 us
    all_to_all x1, starting transfers between devices, local(): lax.all_to_all(back_slots, 'dp', split_axis=0, concat_axis=0, tiled=True)  9.91 us
    all_to_all x1, waiting for transfers between devices, local(): lax.all_to_all(outgoing, 'dp', split_axis=0, concat_axis=0, tiled=True)  9.75 us
    ppermute x2, starting transfers between devices, extended(): lax.ppermute(lax.slice_in_dim(block, 0, width, axis=dim), axis, backward)  8.16 us
    dot_general x1, matrix products, local(): jnp.dot(normed, full_qkv, preferred_element_type=jnp.float32)  5.54 us
    dot_general x2, matrix products, times_out(): jnp.dot(spread(attended, side), out_pairs, preferred_element_type=jnp.flo...  5.18 us
  transfers between devices with their start and end apart: 9, of which 5 were waited for; matrix products, arithmetic and copies ran while one was open for 19% of the time, Pallas kernels for 0%

commit v1 on v0

--- a/solution.py
+++ b/solution.py
@@ -25,8 +25,17 @@
     qkv_rows, qkv_cols = qkv_weight.shape
     out_rows, out_cols = out_weight.shape
     out_wide = out_weight.reshape(qkv_rows, out_rows * out_cols // qkv_rows)
-    both = lax.all_gather(
-        jnp.concatenate([qkv_weight, out_wide], axis=1), "tensor", axis=0, tiled=True
+    both = jnp.concatenate(
+        lax.all_to_all(
+            jnp.stack(
+                lax.psum(1, axis_name="tensor") * [jnp.concatenate([qkv_weight, out_wide], axis=1)],
+                axis=0,
+            ),
+            axis_name="tensor",
+            split_axis=0,
+            concat_axis=0,
+        ),
+        0,
     )
     full_qkv = both[:, :qkv_cols]
     out_pairs = both[:, qkv_cols:]

time: 186 us -> 421 us (2.26)
  waiting for transfers between devices: 70.2 us -> 311 us
  between operations: 15 us -> 1.46 us
  matrix products: 25.7 us -> 33.9 us
  other arithmetic: 19.1 us -> 11.8 us
    ppermute x2, waiting for transfers between devices: 0.01 us -> 268 us  [extended(): lax.ppermute(lax.slice_in_dim(block, 0, width, axis=dim), axis, backward)]
    all_gather x1 -> x0, waiting for transfers between devices: 42 us -> none  [gather_weights(): lax.all_gather(jnp.concatenate([qkv_weight, out_wide], axis=1), 'tensor',...]
    all_to_all x1, waiting for transfers between devices: 9.75 us -> 25.1 us  [local(): lax.all_to_all(outgoing, 'dp', split_axis=0, concat_axis=0, tiled=True)]
    all_to_all x0 -> x1, starting transfers between devices: none -> 10.1 us  [gather_weights(): lax.all_to_all(jnp.stack(lax.psum(1, axis_name='tensor') * [jnp.concatena...]
    another operation x0 -> x1, local copies, waits for them, and re-layouts: none -> 5.88 us  [gather_weights(): jnp.stack(lax.psum(1, axis_name='tensor') * [jnp.concatenate([qkv_weight,...]
    dot_general x2, matrix products: 2.07 us -> 6.77 us  [times_out_t(): lax.dot_general(grad_rows[:, side * half:(side + 1) * half], out_pairs, (...]
    all_to_all x1, starting transfers between devices: 9.91 us -> 5.57 us  [local(): lax.all_to_all(back_slots, 'dp', split_axis=0, concat_axis=0, tiled=True)]
  transfers between devices with their start and end apart: 9 -> 9, of which waited for: 5 -> 6; matrix products, arithmetic and copies ran while one was open for 19% -> 7% of each run, Pallas kernels for 0% -> 0%
where the time goes in v1:
time: 421 us; the launch traced here: 420 us
  waiting for transfers between devices  311 us (74%)
  starting transfers between devices  41.8 us (10%)
  matrix products  33.9 us (8%)
  local copies, waits for them, and re-layouts  19.2 us (5%)
  other arithmetic  11.8 us (3%)
    ppermute x2, waiting for transfers between devices, extended(): lax.ppermute(lax.slice_in_dim(block, 0, width, axis=dim), axis, backward)  268 us
    all_to_all x1, waiting for transfers between devices, local(): lax.all_to_all(outgoing, 'dp', split_axis=0, concat_axis=0, tiled=True)  25.1 us
    all_to_all x1, waiting for transfers between devices, local(): lax.all_to_all(back_slots, 'dp', split_axis=0, concat_axis=0, tiled=True)  11.8 us
    all_to_all x1, starting transfers between devices, local(): lax.all_to_all(outgoing, 'dp', split_axis=0, concat_axis=0, tiled=True)  10.2 us
    all_to_all x1, starting transfers between devices, gather_weights(): lax.all_to_all(jnp.stack(lax.psum(1, axis_name='tensor') * [jnp.concatena...  10.1 us
  transfers between devices with their start and end apart: 9, of which 6 were waited for; matrix products, arithmetic and copies ran while one was open for 7% of the time, Pallas kernels for 0%

profile of v1, /device:TPU:66, one launch (start us, length us, event | category | flops | bytes accessed | tf_op | source)
XLA Modules:
  0.0 419.6 jit_solution(15050894225258487924)
XLA Ops:
  1.8 1.1 gather_fusion.1
  3.0 1.2 reshape.395
  4.2 10.2 %all-to-all-start = ((bf16[32,6,1792]{2,1,0:T(8,128)(2,1)}), bf16[32,6,1792]{2,1,0:T(8,128)(2,1)S(1)}, u32[]{:S(2)}, u32[]{:S(2)}) async-start(bf16[32,6,1792]{2,1,0:T(8,128)(2,1)} %reshape.395), calls=%async_computation | async-start | bytes 1835008 | tf_op jit(solution)/shard_map/all_to_all | solution.py:137
  14.6 25.1 %all-to-all-done = bf16[32,6,1792]{2,1,0:T(8,128)(2,1)S(1)} async-done(((bf16[32,6,1792]{2,1,0:T(8,128)(2,1)}), bf16[32,6,1792]{2,1,0:T(8,128)(2,1)S(1)}, u32[]{:S(2)}, u32[]{:S(2)}) %all-to-all-start) | async-done | bytes 688160 | tf_op jit(solution)/shard_map/all_to_all | solution.py:137
  39.7 5.9 %stack.6 = bf16[16,112,3584]{2,1,0:T(8,128)(2,1)} broadcast(bf16[112,3584]{1,0:T(8,128)(2,1)S(1)} %pad_maximum_fusion.1), dimensions={1,2} | broadcast | bytes 13647872 | tf_op jit(solution)/shard_map/stack | solution.py:30
  45.6 10.1 %all-to-all-start.1 = ((bf16[16,112,3584]{2,1,0:T(8,128)(2,1)}), bf16[16,112,3584]{2,1,0:T(8,128)(2,1)}, u32[]{:S(2)}, u32[]{:S(2)}) async-start(bf16[16,112,3584]{2,1,0:T(8,128)(2,1)} %stack.6), calls=%async_computation.1 | async-start | bytes 25690112 | tf_op jit(solution)/shard_map/all_to_all | solution.py:29
  55.8 2.0 collective-permute-start.1
  57.8 2.3 collective-permute-start
  60.3 1.2 scatter_custom_fusion.1
  64.5 267.7 %collective-permute-done.1 = s32[96]{0:T(128)S(1)} collective-permute-done((s32[96]{0:T(128)S(1)}, s32[96]{0:T(128)S(1)}, u32[]{:S(2)}, u32[]{:S(2)}) %collective-permute-start.1) | collective-permute-done | bytes 416 | tf_op jit(solution)/shard_map/ppermute | solution.py:19
  334.7 5.4 %fusion.9 = bf16[128,2688]{1,0:T(8,128)(2,1)S(1)} fusion(bf16[1792,3584]{1,0:T(8,128)(2,1)} %bitcast.8, f32[1792]{0:T(1024)S(1)} %copy-done.20, f32[128]{0:T(128)S(1)} %add_rsqrt_fusion, f32[128]{0:T(128)S(1)} %broadcast_multiply_fusion.2, bf16[128,1792]{1,0:T(8,128)(2,1)S(1)} %gather_fusion, pred[128]{0:T(512)(128)(4,1)S(1)} %compare_and_fusion.2), kind=kOutput, calls=%fused_computation.15 | convolution fusion | flops 1234845696 | bytes 10788992 | tf_op jit(solution)/shard_map/dot_general | solution.py:150
  340.2 3.8 collective-permute-start.3
  344.0 2.1 collective-permute-start.2
  346.1 2.9 convolution_bitcast_fusion.1
  349.0 3.9 fusion.12
  352.9 1.2 reduce_sum.76
  360.0 3.7 collective-permute-start.4
  363.7 2.0 collective-permute-start.5
  365.9 1.7 fusion.37
  367.6 4.7 %collective-permute-done.4 = f32[96,1792]{1,0:T(8,128)S(1)} collective-permute-done((f32[96,1792]{1,0:T(8,128)S(1)}, f32[96,1792]{1,0:T(8,128)S(1)}, u32[]{:S(2)}, u32[]{:S(2)}) %collective-permute-start.4) | collective-permute-done | bytes 688160 | tf_op jit(solution)/shard_map/ppermute | solution.py:183
  372.5 1.7 collective-permute-done.5
  374.4 7.4 %fusion.106 = (f32[128]{0:T(128)S(1)}, f32[128]{0:T(128)S(1)}, f32[128,1792]{1,0:T(8,128)}) fusion(f32[128]{0:T(128)S(1)} %copy-done.19, f32[128]{0:T(128)S(1)} %copy-done.11, bf16[128,1792]{1,0:T(8,128)(2,1)S(1)} %gather_fusion, pred[128]{0:T(512)(128)(4,1)S(1)} %compare_and_fusion.2, f32[1792]{0:T(1024)S(1)} %copy-done.21, ...), kind=kOutput, calls=%fused_computation.154 | convolution fusion | flops 1236336384 | bytes 11707520 | tf_op jit(solution)/shard_map/dot_general | solution.py:188
  381.8 2.7 scatter_custom_fusion
  384.6 1.2 reshape.404
  385.8 5.6 %all-to-all-start.2 = ((bf16[32,6,1792]{2,1,0:T(8,128)(2,1)}), bf16[32,6,1792]{2,1,0:T(8,128)(2,1)S(1)}, u32[]{:S(2)}, u32[]{:S(2)}) async-start(bf16[32,6,1792]{2,1,0:T(8,128)(2,1)} %reshape.404), calls=%async_computation.2 | async-start | bytes 1835008 | tf_op jit(solution)/shard_map/all_to_all | solution.py:202
  391.4 3.8 fusion.19
  395.2 2.2 reduce_sum.75
  398.2 1.1 fusion.108
  399.3 2.6 fusion.31
  401.9 2.6 fusion.28
  405.5 11.8 %all-to-all-done.2 = bf16[32,6,1792]{2,1,0:T(8,128)(2,1)S(1)} async-done(((bf16[32,6,1792]{2,1,0:T(8,128)(2,1)}), bf16[32,6,1792]{2,1,0:T(8,128)(2,1)S(1)}, u32[]{:S(2)}, u32[]{:S(2)}) %all-to-all-start.2) | async-done | bytes 688160 | tf_op jit(solution)/shard_map/all_to_all | solution.py:202
  417.5 1.1 gather_fusion.2
  (120 shorter events, 16.1 us)
Async XLA Ops:
  3.0 11.4 %copy-start.7 = (bf16[56,1792]{1,0:T(8,128)(2,1)S(1)}, bf16[56,1792]{1,0:T(8,128)(2,1)}, u32[]{:S(2)}) copy-start(bf16[56,1792]{1,0:T(8,128)(2,1)} %param.20) | copy-start | bytes 602116
  3.0 11.5 %copy-start.4 = (bf16[112,2688]{1,0:T(8,128)(2,1)S(1)}, bf16[112,2688]{1,0:T(8,128)(2,1)}, u32[]{:S(2)}) copy-start(bf16[112,2688]{1,0:T(8,128)(2,1)} %param.19) | copy-start | bytes 1806340
  4.2 35.5 %all-to-all-start = ((bf16[32,6,1792]{2,1,0:T(8,128)(2,1)}), bf16[32,6,1792]{2,1,0:T(8,128)(2,1)S(1)}, u32[]{:S(2)}, u32[]{:S(2)}) async-start(bf16[32,6,1792]{2,1,0:T(8,128)(2,1)} %reshape.395), calls=%async_computation | async-start | bytes 1835008 | tf_op jit(solution)/shard_map/all_to_all | solution.py:137
  45.6 10.1 %copy-start.22 = (s32[1,128]{1,0:T(1,128)S(1)}, s32[1,128]{1,0:T(1,128)}, u32[]{:S(2)}) copy-start(s32[1,128]{1,0:T(1,128)} %param.17) | copy-start | bytes 1540
  45.6 15.9 %copy-start.23 = (s32[1,128]{1,0:T(1,128)S(1)}, s32[1,128]{1,0:T(1,128)}, u32[]{:S(2)}) copy-start(s32[1,128]{1,0:T(1,128)} %param.16) | copy-start | bytes 1540
  45.6 289.1 %all-to-all-start.1 = ((bf16[16,112,3584]{2,1,0:T(8,128)(2,1)}), bf16[16,112,3584]{2,1,0:T(8,128)(2,1)}, u32[]{:S(2)}, u32[]{:S(2)}) async-start(bf16[16,112,3584]{2,1,0:T(8,128)(2,1)} %stack.6), calls=%async_computation.1 | async-start | bytes 25690112 | tf_op jit(solution)/shard_map/all_to_all | solution.py:29
  55.8 276.4 %collective-permute-start.1 = (s32[96]{0:T(128)S(1)}, s32[96]{0:T(128)S(1)}, u32[]{:S(2)}, u32[]{:S(2)}) collective-permute-start(s32[96]{0:T(128)S(1)} %get-tuple-element.42), channel_id=1, source_target_pairs={{1,0},{2,1},{3,2},{4,3},{5,4},{6,5},{7,6},{8,7},{9,8},{10,9},{11,1... | collective-permute-start | bytes 1160 | tf_op jit(solution)/shard_map/ppermute | solution.py:19
  57.8 274.9 %collective-permute-start = (s32[96]{0:T(128)S(1)}, s32[96]{0:T(128)S(1)}, u32[]{:S(2)}, u32[]{:S(2)}) collective-permute-start(s32[96]{0:T(128)S(1)} %get-tuple-element.41), channel_id=1, source_target_pairs={{0,1},{1,2},{2,3},{3,4},{4,5},{5,6},{6,7},{7,8},{8,9},{9,10},{10,1... | collective-permute-start | bytes 1160 | tf_op jit(solution)/shard_map/ppermute | solution.py:16
  61.5 292.8 %copy-start.12 = (pred[1024]{0:T(1024)(128)(4,1)}, pred[1024]{0:T(1024)(128)(4,1)S(1)}, u32[]{:S(2)}) copy-start(pred[1024]{0:T(1024)(128)(4,1)S(1)} %fusion.95) | copy-start | bytes 3076
  62.8 291.5 %copy-start.14 = (pred[896]{0:T(1024)(128)(4,1)}, pred[896]{0:T(1024)(128)(4,1)S(1)}, u32[]{:S(2)}) copy-start(pred[896]{0:T(1024)(128)(4,1)S(1)} %fusion.94) | copy-start | bytes 2692
  333.2 1.5 copy-start.20
  334.4 5.7 %copy-start.10 = (f32[128]{0:T(128)}, f32[128]{0:T(128)S(1)}, u32[]{:S(2)}) copy-start(f32[128]{0:T(128)S(1)} %broadcast_multiply_fusion.2) | copy-start | bytes 1540
  334.7 5.4 %copy-start.18 = (f32[128]{0:T(128)}, f32[128]{0:T(128)S(1)}, u32[]{:S(2)}) copy-start(f32[128]{0:T(128)S(1)} %add_rsqrt_fusion) | copy-start | bytes 1540
  340.1 8.9 %copy-start.2 = (bf16[128,2688]{1,0:T(8,128)(2,1)}, bf16[128,2688]{1,0:T(8,128)(2,1)S(1)}, u32[]{:S(2)}) copy-start(bf16[128,2688]{1,0:T(8,128)(2,1)S(1)} %fusion.9) | copy-start | bytes 2064388
  340.2 5.9 %copy-start.5 = (bf16[1,128,1792]{2,1,0:T(8,128)(2,1)S(1)}, bf16[1,128,1792]{2,1,0:T(8,128)(2,1)}, u32[]{:S(2)}) copy-start(bf16[1,128,1792]{2,1,0:T(8,128)(2,1)} %param.21) | copy-start | bytes 1376260
  340.2 15.2 %collective-permute-start.3 = (bf16[96,1792]{1,0:T(8,128)(2,1)S(1)}, bf16[96,1792]{1,0:T(8,128)(2,1)S(1)}, u32[]{:S(2)}, u32[]{:S(2)}) collective-permute-start(bf16[96,1792]{1,0:T(8,128)(2,1)S(1)} %get-tuple-element.36), channel_id=1, source_target_pairs={{1,0},{2,1},{3,2},{4,3},{5,4},{6,5},{7,6},{8,7},{9,8},{10,9},{11,1... | collective-permute-start | bytes 1032200 | tf_op jit(solution)/shard_map/ppermute | solution.py:19
  344.0 11.4 %collective-permute-start.2 = (bf16[96,1792]{1,0:T(8,128)(2,1)S(1)}, bf16[96,1792]{1,0:T(8,128)(2,1)S(1)}, u32[]{:S(2)}, u32[]{:S(2)}) collective-permute-start(bf16[96,1792]{1,0:T(8,128)(2,1)S(1)} %get-tuple-element.35), channel_id=1, source_target_pairs={{0,1},{1,2},{2,3},{3,4},{4,5},{5,6},{6,7},{7,8},{8,9},{9,10},{10,1... | collective-permute-start | bytes 1032200 | tf_op jit(solution)/shard_map/ppermute | solution.py:16
  349.0 5.3 %slice-start.1 = ((bf16[128,2688]{1,0:T(8,128)(2,1)}), bf16[128,896]{1,0:T(8,128)(2,1)S(1)}, s32[]{:S(2)}) async-start(bf16[128,2688]{1,0:T(8,128)(2,1)} %copy-done.2), calls=%async_computation.4 | async-start | bytes 458752 | tf_op jit(solution)/shard_map/slice | solution.py:151
  355.5 3.1 copy-start.3
  359.8 6.0 %slice-start.2 = ((bf16[320,1792]{1,0:T(8,128)(2,1)}), bf16[320,896]{1,0:T(8,128)(2,1)S(1)}, s32[]{:S(2)}) async-start(bf16[320,1792]{1,0:T(8,128)(2,1)} %copy-done.3), calls=%async_computation.5 | async-start | bytes 1146880 | tf_op jit(solution)/shard_map/slice | solution.py:111
  359.9 6.0 %copy-start.8 = (s32[8,320]{0,1:T(8,128)S(1)}, s32[8,320]{0,1:T(8,128)}, u32[]{:S(2)}) copy-start(s32[8,320]{0,1:T(8,128)} %copy.28) | copy-start | bytes 30724
  359.9 6.0 %copy-start.9 = (s32[8,320]{0,1:T(8,128)S(1)}, s32[8,320]{0,1:T(8,128)}, u32[]{:S(2)}) copy-start(s32[8,320]{0,1:T(8,128)} %copy.27) | copy-start | bytes 30724
  359.9 6.0 %copy-start.15 = (pred[896]{0:T(1024)(128)(4,1)S(1)}, pred[896]{0:T(1024)(128)(4,1)}, u32[]{:S(2)}) copy-start(pred[896]{0:T(1024)(128)(4,1)} %copy-done.14) | copy-start | bytes 2692
  360.0 12.4 %collective-permute-start.4 = (f32[96,1792]{1,0:T(8,128)S(1)}, f32[96,1792]{1,0:T(8,128)S(1)}, u32[]{:S(2)}, u32[]{:S(2)}) collective-permute-start(f32[96,1792]{1,0:T(8,128)S(1)} %get-tuple-element.29), channel_id=1, source_target_pairs={{0,1},{1,2},{2,3},{3,4},{4,5},{5,6},{6,7},{7,8},{8,9},{9,10},{10,1... | collective-permute-start | bytes 2064392 | tf_op jit(solution)/shard_map/ppermute | solution.py:183
  363.7 10.5 %collective-permute-start.5 = (f32[96,1792]{1,0:T(8,128)S(1)}, f32[96,1792]{1,0:T(8,128)S(1)}, u32[]{:S(2)}, u32[]{:S(2)}) collective-permute-start(f32[96,1792]{1,0:T(8,128)S(1)} %get-tuple-element.30), channel_id=1, source_target_pairs={{1,0},{2,1},{3,2},{4,3},{5,4},{6,5},{7,6},{8,7},{9,8},{10,9},{11,1... | collective-permute-start | bytes 2064392 | tf_op jit(solution)/shard_map/ppermute | solution.py:184
  372.5 1.9 copy-start.11
  372.5 1.9 copy-start.19
  372.5 1.9 copy-start.21
  374.4 7.5 %copy-start.6 = (bf16[1,128,1792]{2,1,0:T(8,128)(2,1)S(1)}, bf16[1,128,1792]{2,1,0:T(8,128)(2,1)}, u32[]{:S(2)}) copy-start(bf16[1,128,1792]{2,1,0:T(8,128)(2,1)} %param.21) | copy-start | bytes 1376260
  384.6 6.8 %copy-start.13 = (pred[1024]{0:T(1024)(128)(4,1)S(1)}, pred[1024]{0:T(1024)(128)(4,1)}, u32[]{:S(2)}) copy-start(pred[1024]{0:T(1024)(128)(4,1)} %copy-done.12) | copy-start | bytes 3076
  385.8 31.5 %all-to-all-start.2 = ((bf16[32,6,1792]{2,1,0:T(8,128)(2,1)}), bf16[32,6,1792]{2,1,0:T(8,128)(2,1)S(1)}, u32[]{:S(2)}, u32[]{:S(2)}) async-start(bf16[32,6,1792]{2,1,0:T(8,128)(2,1)} %reshape.404), calls=%async_computation.2 | async-start | bytes 1835008 | tf_op jit(solution)/shard_map/all_to_all | solution.py:202
  417.5 2.1 copy-start.1
  (4 other events, 3.9 us)
